TPU v7x, 512 devices: a whole 4x8x8 slice. The times are simulated.
512 devices in a mesh: dp: 2 (over core), section: 4 (over x), expert: 64 (over y, z).
Axes of the slice: x: 4, y: 8, z: 8, core: 2. Of those that a mesh axis runs over, the one named last changes fastest.
Arguments:
- grad_out: bfloat16 [16384, 3584], P(('dp', 'expert'), 'section'), may hold values from -6 to 6
- expert_ids: int32 [16384, 8], P(('dp', 'expert')), may hold values from 0 to 63, all different within a row; in each aligned block of 128 rows (0 to 127, 128 to 255, ...) at most 24 rows name the same one
- gate_weights: float32 [16384, 8], P(('dp', 'expert')), may hold values from 0.1 to 1
- act: bfloat16 [16384, 8, 1024], P(('dp', 'expert'), None, 'section'), may hold values from -0.8984375 to 0.8984375
- w_down: bfloat16 [64, 1024, 3584], P('expert', 'section'), may hold values from -0.09375 to 0.09375
Outputs:
- grad_hidden: bfloat16 [16384, 8, 1024], P(('dp', 'expert'), None, 'section')
- grad_gates: float32 [16384, 8], P(('dp', 'expert'))
- grad_w: bfloat16 [64, 1024, 3584], P('expert', 'section', 'dp')
Inputs may be any that keep to these rules, and one draw needn't show every extreme that they name: `expert_ids`: each row names 8 different experts. In each aligned block of 128 rows (the tokens of one device) no expert is named by more than 24 rows, and in every draw some expert is named by exactly 24 rows of some block.
All inputs are finite; a program needn't handle non-finite values.
Results may differ from a plain program's by a relative error of at most 0.0058.
Values may be sent and summed in bfloat16 or wider, within the bound.
No kernel may reach another device: no remote copies, remote signals or barrier semaphores. Data moves between devices by JAX's collectives and lax.ppermute only.
A program may use at most 64 MiB of HBM per device.

v0:
```python
import jax
import jax.numpy as jnp
from jax import lax
from jax.sharding import PartitionSpec as P


def routing(expert_ids, experts, capacity):
    tok_count, top_count = expert_ids.shape
    onehot = expert_ids[:, :, None] == jnp.arange(experts, dtype=jnp.int32)[None, None, :]
    per_token = jnp.any(onehot, axis=1).astype(jnp.bfloat16)
    rows = jnp.arange(tok_count, dtype=jnp.int32)
    lower = (rows[:, None] > rows[None, :]).astype(jnp.bfloat16)
    before = jnp.dot(lower, per_token, preferred_element_type=jnp.float32)
    order_in = jnp.sum(jnp.where(onehot, before[:, None, :], 0.0), axis=2).astype(jnp.int32)
    position = expert_ids * capacity + order_in
    slots = jnp.arange(experts * capacity, dtype=jnp.int32)
    sel_pairs = position.reshape(tok_count * top_count)[None, :] == slots[:, None]
    pairs = jnp.arange(tok_count * top_count, dtype=jnp.int32)
    member = (pairs[:, None] // top_count == rows[None, :]).astype(jnp.bfloat16)
    sel_pairs = sel_pairs.astype(jnp.bfloat16)
    sel_tok = jnp.dot(sel_pairs, member, preferred_element_type=jnp.float32).astype(jnp.bfloat16)
    return (sel_pairs, sel_tok)


def local(grad_out, expert_ids, gate_weights, act, w_down):
    tok_count, top_count = expert_ids.shape
    hidden_slice = act.shape[2]
    d_slice = grad_out.shape[1]
    n_expert = lax.axis_size("expert")
    n_section = lax.axis_size("section")
    experts = w_down.shape[0] * n_expert
    capacity = 3 * tok_count * top_count // (2 * experts)
    pair_count = tok_count * top_count
    slot_count = experts * capacity
    sel_pairs, sel_tok = routing(expert_ids, experts, capacity)
    scaled = (
        (gate_weights[:, :, None] * act.astype(jnp.float32))
        .astype(jnp.bfloat16)
        .reshape(pair_count, hidden_slice)
    )
    send_scaled = jnp.dot(sel_pairs, scaled, preferred_element_type=jnp.float32).astype(
        jnp.bfloat16
    )
    send_grad = jnp.dot(sel_tok, grad_out, preferred_element_type=jnp.float32).astype(jnp.bfloat16)
    send = jnp.concatenate([send_grad, send_scaled], axis=1).reshape(
        experts, capacity, d_slice + hidden_slice
    )
    w_local = w_down[0].reshape(hidden_slice, n_section, d_slice)
    recv = lax.all_to_all(send, "expert", split_axis=0, concat_axis=0, tiled=True)
    recv = recv.reshape(slot_count, d_slice + hidden_slice)
    half = slot_count // 2
    first = recv[:half]
    second = recv[half:]
    gathered_first = lax.all_gather(first[:, :d_slice], "section", axis=0, tiled=False)
    spread = jnp.broadcast_to(second[None, :, :d_slice], (n_section, slot_count - half, d_slice))
    gathered_second = lax.all_to_all(spread, "section", split_axis=0, concat_axis=0, tiled=True)
    received = [(first[:, d_slice:], gathered_first), (second[:, d_slice:], gathered_second)]
    weight_acc = None
    returning = []
    for recv_scaled, gathered in received:
        unscaled = jnp.einsum("srd,hsd->rh", gathered, w_local, preferred_element_type=jnp.float32)
        returning.append(unscaled.astype(jnp.bfloat16))
        term = jnp.einsum("rh,srd->hsd", recv_scaled, gathered, preferred_element_type=jnp.float32)
        weight_acc = term if weight_acc is None else weight_acc + term
    weight_part = weight_acc.astype(jnp.bfloat16).reshape(1, hidden_slice, n_section * d_slice)
    grad_w = lax.psum_scatter(weight_part, "dp", scatter_dimension=2, tiled=True)
    returning = jnp.concatenate(returning, axis=0).reshape(experts, capacity, hidden_slice)
    returned = lax.all_to_all(returning, "expert", split_axis=0, concat_axis=0, tiled=True)
    unscaled_tok = lax.dot_general(
        sel_pairs,
        returned.reshape(slot_count, hidden_slice),
        (((0,), (0,)), ((), ())),
        preferred_element_type=jnp.float32,
    ).reshape(tok_count, top_count, hidden_slice)
    grad_hidden = (gate_weights[:, :, None] * unscaled_tok).astype(jnp.bfloat16)
    gate_share = jnp.sum(act.astype(jnp.float32) * unscaled_tok, axis=2)
    grad_gates = lax.psum(gate_share, "section")
    return (grad_hidden, grad_gates, grad_w)


def solution(mesh):
    placed = (
        P(("dp", "expert"), "section"),
        P(("dp", "expert"), None),
        P(("dp", "expert"), None),
        P(("dp", "expert"), None, "section"),
        P("expert", "section", None),
    )
    return jax.shard_map(
        local,
        mesh=mesh,
        in_specs=placed,
        out_specs=(
            P(("dp", "expert"), None, "section"),
            P(("dp", "expert"), None),
            P("expert", "section", "dp"),
        ),
        check_vma=False,
    )
```

profile of v0, /device:TPU:18, one launch (start us, length us, event | category | flops | bytes accessed | tf_op | source)
XLA Modules:
  0.0 324.6 jit_solution(13033326550447104199)
XLA Ops:
  7.2 0.0 copy-start
  7.2 0.0 all-gather.3.cloned.1.call-start
  7.2 0.8 fusion.33
  8.0 0.1 fusion.34
  8.1 0.7 select_reduce_fusion
  8.9 0.7 convert_add_fusion
  9.6 0.1 copy.29
  9.7 0.1 eq.67
  9.8 1.3 fusion.26
  11.1 2.5 fusion.8
  13.5 0.0 copy-done
  13.5 2.9 convolution_convert_fusion
  16.5 3.1 pad_maximum_fusion
  19.6 5.8 %copy.32 = bf16[1536,1152]{1,0:T(8,128)(2,1)} copy(bf16[1536,1152]{0,1:T(8,128)(2,1)} %pad_maximum_fusion) | data formatting | bytes 7077888 | tf_op jit(solution)/shard_map/concatenate | solution.py:45
  25.4 99.4 %all_to_all.15 = bf16[64,24,1152]{2,1,0:T(8,128)(2,1)S(1)} all-to-all(bf16[64,24,1152]{2,1,0:T(8,128)(2,1)} %bitcast.40), channel_id=1, replica_groups=mesh['dp'=2,'section'=4,'expert'=64] {'expert'}, dimensions={0} | all-to-all | bytes 7077888 | tf_op jit(solution)/shard_map/all_to_all | solution.py:49
  124.8 0.3 fusion.38
  125.0 0.0 copy-start.2
  125.1 0.0 copy-start.1
  125.1 1.3 copy-done.2
  126.3 1.2 slice.33
  127.5 0.0 all-gather.3.cloned.1.call-update
  127.5 0.1 slice.35
  127.7 2.8 broadcast_in_dim.16
  130.4 0.0 copy-done.1
  130.4 5.6 %all-to-all-start.1 = ((bf16[4,768,896]{2,1,0:T(8,128)(2,1)}), bf16[4,768,896]{2,1,0:T(8,128)(2,1)}, u32[]{:S(2)}, u32[]{:S(2)}) async-start(bf16[4,768,896]{2,1,0:T(8,128)(2,1)} %broadcast_in_dim.16), calls=%async_computation.1 | async-start | bytes 11010048 | tf_op jit(solution)/shard_map/all_to_all | solution.py:56
  136.1 0.0 reduce-scatter.2.cloned.1.call-start
  136.1 102.4 %all-gather.3.cloned.1.call-done = bf16[3072,896]{1,0:T(8,128)(2,1)} async-done(((bf16[768,896]{1,0:T(8,128)(2,1)}), bf16[3072,896]{1,0:T(8,128)(2,1)}) %all-gather.3.cloned.1.call-update) | async-done | bytes 5505040 | tf_op jit(solution)/shard_map/all_gather | solution.py:54
  238.4 6.1 %fusion.30 = f32[256,4,896]{2,0,1:T(8,128)} fusion(bf16[4,768,896]{2,1,0:T(8,128)(2,1)} %bitcast.46, bf16[768,1152]{1,0:T(8,128)(2,1)} %bitcast.45), kind=kOutput, calls=%fused_computation.33 | convolution fusion | flops 1409286144 | bytes 9568256 | tf_op jit(solution)/shard_map/rh,srd->hsd/dot_general | solution.py:63
  244.5 0.0 all-to-all-done.1
  244.6 5.4 %add_convert_fusion = bf16[256,4,896]{2,0,1:T(8,128)(2,1)S(1)} fusion(f32[256,4,896]{2,0,1:T(8,128)} %fusion.30, bf16[4,768,896]{2,1,0:T(8,128)(2,1)} %all-to-all-done.1, bf16[768,1152]{1,0:T(8,128)(2,1)} %bitcast.43), kind=kOutput, calls=%fused_computation.6 | convolution fusion | flops 1411121152 | bytes 11403264 | tf_op jit(solution)/shard_map/rh,srd->hsd/dot_general | solution.py:63
  250.0 2.4 copy.37
  252.4 0.0 reduce-scatter.2.cloned.1.call-update
  252.4 0.0 slice-start
  252.4 3.4 %reshape_squeeze.3 = bf16[256,4,896]{2,1,0:T(4,128)(2,1)S(1)} reshape(bf16[1,256,3584]{2,1,0:T(8,128)(2,1)} %param.9) | data formatting | bytes 3670016 | tf_op jit(solution)/shard_map/reshape;squeeze | solution.py:48
  255.9 0.0 slice-start.1
  255.9 4.3 %fusion.20 = bf16[768,256]{1,0:T(8,128)(2,1)S(1)} fusion(bf16[4,768,896]{2,1,0:T(8,128)(2,1)} %all-to-all-done.1, bf16[256,4,896]{2,1,0:T(4,128)(2,1)S(1)} %reshape_squeeze.3), kind=kOutput, calls=%fused_computation.22 | convolution fusion | flops 1409482752 | bytes 7733248 | tf_op jit(solution)/shard_map/srd,hsd->rh/dot_general | solution.py:61
  260.2 0.0 slice-done
  260.2 0.0 slice-done.1
  260.2 0.0 copy-start.3
  260.3 0.0 copy-start.4
  260.3 1.6 fusion.23
  261.9 0.1 pad_maximum_fusion.1
  262.0 38.3 %all_to_all.16 = bf16[64,24,256]{2,1,0:T(8,128)(2,1)S(1)} all-to-all(bf16[64,24,256]{2,1,0:T(8,128)(2,1)S(1)} %bitcast.50), channel_id=1, replica_groups=mesh['dp'=2,'section'=4,'expert'=64] {'expert'}, dimensions={0} | all-to-all | bytes 1572864 | tf_op jit(solution)/shard_map/all_to_all | solution.py:68
  300.2 0.0 copy-done.3
  300.2 0.0 copy-done.4
  300.2 1.4 fusion.27
  301.6 1.1 copy.38
  302.7 12.8 %psum.7 = f32[128,8]{0,1:T(8,128)} all-reduce(f32[128,8]{0,1:T(8,128)S(1)} %get-tuple-element.14), channel_id=1, replica_groups=mesh['dp'=2,'section'=4,'expert'=64] {'section'}, use_global_device_ids=true, to_apply=%region_3.4 | all-reduce | flops 1024 | bytes 8192 | tf_op jit(solution)/shard_map/psum | solution.py:77
  315.6 0.0 reduce-scatter.2.cloned.1.call-done
  315.6 2.2 copy.39
  (2 shorter events, 0.0 us)
Async XLA Ops:
  7.2 6.4 %copy-start = (bf16[128,896]{1,0:T(8,128)(2,1)S(1)}, bf16[128,896]{1,0:T(8,128)(2,1)}, u32[]{:S(2)}) copy-start(bf16[128,896]{1,0:T(8,128)(2,1)} %param.5) | copy-start | bytes 688132
  7.2 231.2 %all-gather.3.cloned.1.call-start = ((), (), s32[]{:S(2)}) async-start(), calls=%async_computation.5 | async-start | bytes 6881280 | tf_op jit(solution)/shard_map/all_gather | solution.py:54
  125.0 1.3 copy-start.2
  125.1 5.4 %copy-start.1 = (bf16[32,24,1152]{2,1,0:T(8,128)(2,1)}, bf16[32,24,1152]{2,1,0:T(8,128)(2,1)S(1)}, u32[]{:S(2)}) copy-start(bf16[32,24,1152]{2,1,0:T(8,128)(2,1)S(1)} %get-tuple-element.13) | copy-start | bytes 5308420
  130.4 114.1 %all-to-all-start.1 = ((bf16[4,768,896]{2,1,0:T(8,128)(2,1)}), bf16[4,768,896]{2,1,0:T(8,128)(2,1)}, u32[]{:S(2)}, u32[]{:S(2)}) async-start(bf16[4,768,896]{2,1,0:T(8,128)(2,1)} %broadcast_in_dim.16), calls=%async_computation.1 | async-start | bytes 11010048 | tf_op jit(solution)/shard_map/all_to_all | solution.py:56
  136.1 179.5 %reduce-scatter.2.cloned.1.call-start = ((), (), s32[]{:S(2)}) async-start(), calls=%async_computation.4 | async-start | bytes 2752512 | tf_op jit(solution)/shard_map/reduce_scatter | solution.py:66
  252.4 7.8 %slice-start = ((s8[5505024]{0:T(1024)(128)(4,1)}), s8[1310720]{0:T(1024)(128)(4,1)S(1)}, s32[]{:S(2)}) async-start(s8[5505024]{0:T(1024)(128)(4,1)} %bitcast.47), calls=%async_computation.6 | async-start | bytes 2621440
  255.9 4.4 %slice-start.1 = ((s8[5505024]{0:T(1024)(128)(4,1)}), s8[4194304]{0:T(1024)(128)(4,1)S(1)}, s32[]{:S(2)}) async-start(s8[5505024]{0:T(1024)(128)(4,1)} %bitcast.47), calls=%async_computation.7 | async-start | bytes 8388608
  260.2 40.0 %copy-start.3 = (bf16[128,8,256]{2,1,0:T(8,128)(2,1)S(1)}, bf16[128,8,256]{2,1,0:T(8,128)(2,1)}, u32[]{:S(2)}) copy-start(bf16[128,8,256]{2,1,0:T(8,128)(2,1)} %param.8) | copy-start | bytes 1572868
  260.3 40.0 %copy-start.4 = (f32[128,8]{0,1:T(8,128)S(1)}, f32[128,8]{0,1:T(8,128)}, u32[]{:S(2)}) copy-start(f32[128,8]{0,1:T(8,128)} %param.7) | copy-start | bytes 12292
Sparse Core Ops, SparseCore 0:
  127.7 110.7 all-gather.2
  252.6 22.7 reduce-scatter.1
where the time goes:
time: 325 us
  blocking collectives  151 us (46%)
  waiting for transfers between devices  102 us (31%)
  matrix products  24.5 us (8%)
  local copies, waits for them, and re-layouts  20.8 us (6%)
  between operations  14.2 us (4%)
  other arithmetic  6.64 us (2%)
  starting transfers between devices  5.67 us (2%)
    all_gather x1, waiting for transfers between devices, local(): lax.all_gather(first[:, :d_slice], 'section', axis=0, tiled=False)  102 us
    all_to_all x1, blocking collectives, local(): lax.all_to_all(send, 'expert', split_axis=0, concat_axis=0, tiled=True)  99.4 us
    all_to_all x1, blocking collectives, local(): lax.all_to_all(returning, 'expert', split_axis=0, concat_axis=0, tiled=True)  38.3 us
    psum x1, blocking collectives, local(): grad_gates = lax.psum(gate_share, 'section')  12.8 us
    dot_general x2, matrix products, local(): jnp.einsum('rh,srd->hsd', recv_scaled, gathered, preferred_element_type=j...  11.5 us
  transfers between devices with their start and end apart: 3, of which 1 were waited for; matrix products, arithmetic and copies ran while one was open for 6% of the time, Pallas kernels for 0%

commit v1 on v0

--- a/solution.py
+++ b/solution.py
@@ -2,6 +2,16 @@
 import jax.numpy as jnp
 from jax import lax
 from jax.sharding import PartitionSpec as P
+
+
+def _report_stops_all(arr, link_axis):
+    long_array = arr
+    n_slots = lax.axis_size(link_axis)
+    for pp in [at for at in (1, 2, 4, 8, 16) if at < n_slots]:
+        long_array = long_array + lax.ppermute(
+            long_array, link_axis, [(w, w ^ pp) for w in range(n_slots)]
+        )
+    return long_array
 
 
 def routing(expert_ids, experts, capacity):
@@ -74,7 +84,7 @@
     ).reshape(tok_count, top_count, hidden_slice)
     grad_hidden = (gate_weights[:, :, None] * unscaled_tok).astype(jnp.bfloat16)
     gate_share = jnp.sum(act.astype(jnp.float32) * unscaled_tok, axis=2)
-    grad_gates = lax.psum(gate_share, "section")
+    grad_gates = _report_stops_all(gate_share, "section")
     return (grad_hidden, grad_gates, grad_w)
 
 

time: 325 us -> 328 us (level)
  the two profiles are of different devices: /device:TPU:18 before, /device:TPU:20 now
where the time goes in v1:
time: 328 us; the launch traced here: 327 us
  blocking collectives  141 us (43%)
  waiting for transfers between devices  111 us (34%)
  matrix products  24.4 us (7%)
  local copies, waits for them, and re-layouts  20.7 us (6%)
  between operations  14.2 us (4%)
  starting transfers between devices  9.45 us (3%)
  other arithmetic  7.23 us (2%)
    all_gather x1, waiting for transfers between devices, local(): lax.all_gather(first[:, :d_slice], 'section', axis=0, tiled=False)  103 us
    all_to_all x1, blocking collectives, local(): lax.all_to_all(send, 'expert', split_axis=0, concat_axis=0, tiled=True)  99.4 us
    all_to_all x1, blocking collectives, local(): lax.all_to_all(returning, 'expert', split_axis=0, concat_axis=0, tiled=True)  41.2 us
    dot_general x2, matrix products, local(): jnp.einsum('rh,srd->hsd', recv_scaled, gathered, preferred_element_type=j...  11.5 us
    ppermute x2, waiting for transfers between devices, _report_stops_all(): lax.ppermute(long_array, link_axis, [(w, w ^ pp) for w in range(n_slots)])  7.56 us
  transfers between devices with their start and end apart: 5, of which 3 were waited for; matrix products, arithmetic and copies ran while one was open for 7% of the time, Pallas kernels for 0%

profile of v1, /device:TPU:20, one launch (start us, length us, event | category | flops | bytes accessed | tf_op | source)
XLA Modules:
  0.0 327.4 jit_solution(318271343807478779)
XLA Ops:
  7.2 0.0 copy-start
  7.2 0.0 all-gather.3.cloned.1.call-start
  7.2 0.8 fusion.33
  8.0 0.1 fusion.34
  8.1 0.7 select_reduce_fusion
  8.9 0.7 convert_add_fusion
  9.6 0.1 copy.29
  9.7 0.1 eq.67
  9.8 1.3 fusion.26
  11.1 2.5 fusion.8
  13.5 0.0 copy-done
  13.5 2.9 convolution_convert_fusion
  16.5 3.1 pad_maximum_fusion
  19.6 5.8 %copy.32 = bf16[1536,1152]{1,0:T(8,128)(2,1)} copy(bf16[1536,1152]{0,1:T(8,128)(2,1)} %pad_maximum_fusion) | data formatting | bytes 7077888 | tf_op jit(solution)/shard_map/concatenate | solution.py:55
  25.4 99.4 %all_to_all.15 = bf16[64,24,1152]{2,1,0:T(8,128)(2,1)S(1)} all-to-all(bf16[64,24,1152]{2,1,0:T(8,128)(2,1)} %bitcast.40), channel_id=1, replica_groups=mesh['dp'=2,'section'=4,'expert'=64] {'expert'}, dimensions={0} | all-to-all | bytes 7077888 | tf_op jit(solution)/shard_map/all_to_all | solution.py:59
  124.8 0.3 fusion.38
  125.1 0.0 copy-start.2
  125.1 0.0 copy-start.1
  125.1 1.2 copy-done.2
  126.3 1.2 slice.33
  127.5 0.0 all-gather.3.cloned.1.call-update
  127.5 0.1 slice.35
  127.6 2.8 broadcast_in_dim.16
  130.4 0.0 copy-done.1
  130.4 5.6 %all-to-all-start.1 = ((bf16[4,768,896]{2,1,0:T(8,128)(2,1)}), bf16[4,768,896]{2,1,0:T(8,128)(2,1)}, u32[]{:S(2)}, u32[]{:S(2)}) async-start(bf16[4,768,896]{2,1,0:T(8,128)(2,1)} %broadcast_in_dim.16), calls=%async_computation.1 | async-start | bytes 11010048 | tf_op jit(solution)/shard_map/all_to_all | solution.py:66
  136.0 0.0 reduce-scatter.2.cloned.1.call-start
  136.0 103.2 %all-gather.3.cloned.1.call-done = bf16[3072,896]{1,0:T(8,128)(2,1)} async-done(((bf16[768,896]{1,0:T(8,128)(2,1)}), bf16[3072,896]{1,0:T(8,128)(2,1)}) %all-gather.3.cloned.1.call-update) | async-done | bytes 5505040 | tf_op jit(solution)/shard_map/all_gather | solution.py:64
  239.1 6.1 %fusion.30 = f32[256,4,896]{2,0,1:T(8,128)} fusion(bf16[4,768,896]{2,1,0:T(8,128)(2,1)} %bitcast.46, bf16[768,1152]{1,0:T(8,128)(2,1)} %bitcast.45), kind=kOutput, calls=%fused_computation.33 | convolution fusion | flops 1409286144 | bytes 9568256 | tf_op jit(solution)/shard_map/rh,srd->hsd/dot_general | solution.py:73
  245.2 0.0 all-to-all-done.1
  245.2 5.4 %add_convert_fusion = bf16[256,4,896]{2,0,1:T(8,128)(2,1)S(1)} fusion(f32[256,4,896]{2,0,1:T(8,128)} %fusion.30, bf16[4,768,896]{2,1,0:T(8,128)(2,1)} %all-to-all-done.1, bf16[768,1152]{1,0:T(8,128)(2,1)} %bitcast.43), kind=kOutput, calls=%fused_computation.6 | convolution fusion | flops 1411121152 | bytes 11403264 | tf_op jit(solution)/shard_map/rh,srd->hsd/dot_general | solution.py:73
  250.7 2.4 copy.37
  253.1 0.0 reduce-scatter.2.cloned.1.call-update
  253.1 0.0 slice-start
  253.1 3.4 %reshape_squeeze.3 = bf16[256,4,896]{2,1,0:T(4,128)(2,1)S(1)} reshape(bf16[1,256,3584]{2,1,0:T(8,128)(2,1)} %param.9) | data formatting | bytes 3670016 | tf_op jit(solution)/shard_map/reshape;squeeze | solution.py:58
  256.5 0.0 slice-start.1
  256.6 4.3 %fusion.20 = bf16[768,256]{1,0:T(8,128)(2,1)S(1)} fusion(bf16[4,768,896]{2,1,0:T(8,128)(2,1)} %all-to-all-done.1, bf16[256,4,896]{2,1,0:T(4,128)(2,1)S(1)} %reshape_squeeze.3), kind=kOutput, calls=%fused_computation.22 | convolution fusion | flops 1409482752 | bytes 7733248 | tf_op jit(solution)/shard_map/srd,hsd->rh/dot_general | solution.py:71
  260.9 0.0 slice-done
  260.9 0.0 slice-done.1
  260.9 0.0 copy-start.3
  260.9 0.0 copy-start.4
  260.9 1.6 fusion.23
  262.6 0.1 pad_maximum_fusion.1
  262.6 41.2 %all_to_all.16 = bf16[64,24,256]{2,1,0:T(8,128)(2,1)S(1)} all-to-all(bf16[64,24,256]{2,1,0:T(8,128)(2,1)S(1)} %bitcast.50), channel_id=1, replica_groups=mesh['dp'=2,'section'=4,'expert'=64] {'expert'}, dimensions={0} | all-to-all | bytes 1572864 | tf_op jit(solution)/shard_map/all_to_all | solution.py:78
  303.8 0.0 copy-done.3
  303.8 0.0 copy-done.4
  303.8 1.4 fusion.27
  305.2 1.9 collective-permute-start
  307.1 3.6 %collective-permute-done = f32[128,8]{0,1:T(8,128)S(1)} collective-permute-done((f32[128,8]{0,1:T(8,128)S(1)}, f32[128,8]{0,1:T(8,128)S(1)}, u32[]{:S(2)}, u32[]{:S(2)}) %collective-permute-start) | collective-permute-done | bytes 4128 | tf_op jit(solution)/shard_map/ppermute | solution.py:11
  310.7 1.9 collective-permute-start.1
  312.6 1.1 copy.38
  313.7 4.0 %collective-permute-done.1 = f32[128,8]{0,1:T(8,128)S(1)} collective-permute-done((f32[128,8]{0,1:T(8,128)S(1)}, f32[128,8]{0,1:T(8,128)S(1)}, u32[]{:S(2)}, u32[]{:S(2)}) %collective-permute-start.1) | collective-permute-done | bytes 4128 | tf_op jit(solution)/shard_map/ppermute | solution.py:11
  317.7 0.6 add.22
  318.3 0.0 reduce-scatter.2.cloned.1.call-done
  318.3 2.2 copy.39
  (3 shorter events, 0.0 us)
Async XLA Ops:
  7.2 6.4 %copy-start = (bf16[128,896]{1,0:T(8,128)(2,1)S(1)}, bf16[128,896]{1,0:T(8,128)(2,1)}, u32[]{:S(2)}) copy-start(bf16[128,896]{1,0:T(8,128)(2,1)} %param.5) | copy-start | bytes 688132
  7.2 232.0 %all-gather.3.cloned.1.call-start = ((), (), s32[]{:S(2)}) async-start(), calls=%async_computation.5 | async-start | bytes 6881280 | tf_op jit(solution)/shard_map/all_gather | solution.py:64
  125.1 1.2 copy-start.2
  125.1 5.3 %copy-start.1 = (bf16[32,24,1152]{2,1,0:T(8,128)(2,1)}, bf16[32,24,1152]{2,1,0:T(8,128)(2,1)S(1)}, u32[]{:S(2)}) copy-start(bf16[32,24,1152]{2,1,0:T(8,128)(2,1)S(1)} %get-tuple-element.13) | copy-start | bytes 5308420
  130.4 114.8 %all-to-all-start.1 = ((bf16[4,768,896]{2,1,0:T(8,128)(2,1)}), bf16[4,768,896]{2,1,0:T(8,128)(2,1)}, u32[]{:S(2)}, u32[]{:S(2)}) async-start(bf16[4,768,896]{2,1,0:T(8,128)(2,1)} %broadcast_in_dim.16), calls=%async_computation.1 | async-start | bytes 11010048 | tf_op jit(solution)/shard_map/all_to_all | solution.py:66
  136.0 182.3 %reduce-scatter.2.cloned.1.call-start = ((), (), s32[]{:S(2)}) async-start(), calls=%async_computation.4 | async-start | bytes 2752512 | tf_op jit(solution)/shard_map/reduce_scatter | solution.py:76
  253.1 7.8 %slice-start = ((s8[5505024]{0:T(1024)(128)(4,1)}), s8[1310720]{0:T(1024)(128)(4,1)S(1)}, s32[]{:S(2)}) async-start(s8[5505024]{0:T(1024)(128)(4,1)} %bitcast.47), calls=%async_computation.6 | async-start | bytes 2621440
  256.5 4.4 %slice-start.1 = ((s8[5505024]{0:T(1024)(128)(4,1)}), s8[4194304]{0:T(1024)(128)(4,1)S(1)}, s32[]{:S(2)}) async-start(s8[5505024]{0:T(1024)(128)(4,1)} %bitcast.47), calls=%async_computation.7 | async-start | bytes 8388608
  260.9 42.9 %copy-start.3 = (bf16[128,8,256]{2,1,0:T(8,128)(2,1)S(1)}, bf16[128,8,256]{2,1,0:T(8,128)(2,1)}, u32[]{:S(2)}) copy-start(bf16[128,8,256]{2,1,0:T(8,128)(2,1)} %param.8) | copy-start | bytes 1572868
  260.9 42.9 %copy-start.4 = (f32[128,8]{0,1:T(8,128)S(1)}, f32[128,8]{0,1:T(8,128)}, u32[]{:S(2)}) copy-start(f32[128,8]{0,1:T(8,128)} %param.7) | copy-start | bytes 12292
  305.2 5.5 %collective-permute-start = (f32[128,8]{0,1:T(8,128)S(1)}, f32[128,8]{0,1:T(8,128)S(1)}, u32[]{:S(2)}, u32[]{:S(2)}) collective-permute-start(f32[128,8]{0,1:T(8,128)S(1)} %get-tuple-element.14), channel_id=1, source_target_pairs={{0,64},{64,0},{128,192},{192,128},{1,65},{65,1},{129,193},{193,129... | collective-permute-start | bytes 12296 | tf_op jit(solution)/shard_map/ppermute | solution.py:11
  310.7 7.0 %collective-permute-start.1 = (f32[128,8]{0,1:T(8,128)S(1)}, f32[128,8]{0,1:T(8,128)S(1)}, u32[]{:S(2)}, u32[]{:S(2)}) collective-permute-start(f32[128,8]{0,1:T(8,128)S(1)} %add.21), channel_id=1, source_target_pairs={{0,128},{64,192},{128,0},{192,64},{1,129},{65,193},{129,1},{193,65... | collective-permute-start | bytes 12296 | tf_op jit(solution)/shard_map/ppermute | solution.py:11
Sparse Core Ops, SparseCore 0:
  127.6 111.4 all-gather.2
  253.2 21.9 reduce-scatter.1
